TPU v7x, 128 devices: a whole 4x4x4 slice. The times are simulated.
128 devices in a mesh: gx: 16 (over z, x), gy: 8 (over y, core).
Axes of the slice: x: 4, y: 4, z: 4, core: 2. Of those that a mesh axis runs over, the one named last changes fastest.
Arguments:
- tokens: bfloat16 [2048, 8192], P('gy', 'gx'), may hold values from -6 to 6
- gate_base_weight: bfloat16 [8192, 29568], P('gx', 'gy'), may hold values from -0.0625 to 0.0625
- up_base_weight: bfloat16 [8192, 29568], P('gx', 'gy'), may hold values from -0.0625 to 0.0625
- adapter_down_maps: bfloat16 [128, 8192, 128], P(('gx', 'gy')), may hold values from -0.0625 to 0.0625
- adapter_up_maps: bfloat16 [128, 128, 29568], P(('gx', 'gy')), may hold values from -0.75 to 0.75
- tenant: int32 [2048, 1], replicated, may hold values from 0 to 127; in each aligned block of 128 rows (0 to 127, 128 to 255, ...) at most 4 rows name the same one
- tenant_slot_index: int32 [128], replicated, may hold values from 0 to 127, as said below
Outputs:
- hidden: bfloat16 [2048, 29568], P('gx', 'gy')
Inputs may be any that keep to these rules, and one draw needn't show every extreme that they name: In each aligned block of 128 rows no tenant names more than 4 rows, and in some block a tenant names exactly 4. `tenant_slot_index`: A permutation of the slots; slot s is held by device s of gx+gy, gx the slower index.
All inputs are finite; a program needn't handle non-finite values.
Results may differ from a plain program's by a relative error of at most 0.019.
Values may be sent and summed in bfloat16 or wider, within the bound.
No kernel may reach another device: no remote copies, remote signals or barrier semaphores. Data moves between devices by JAX's collectives and lax.ppermute only.
A program may use at most 192 MiB of HBM per device.

v0:
```python
import jax
import jax.numpy as jnp
from jax import lax
from jax.sharding import PartitionSpec as P

CAP = 4


def body(
    tokens,
    gate_base_weight,
    up_base_weight,
    adapter_down_maps,
    adapter_up_maps,
    tenant,
    tenant_slot_index,
):
    tile_grid_rows = lax.axis_size("gx")
    tile_grid_columns = lax.axis_size("gy")
    devices = tile_grid_rows * tile_grid_columns
    row_gx = lax.axis_index("gx")
    row_gy = lax.axis_index("gy")
    local_rows = tokens.shape[0]
    tile_width = tokens.shape[1]
    total_rows = tenant.shape[0]
    block = total_rows // tile_grid_rows
    groups = local_rows // block
    tenants = tenant_slot_index.shape[0]
    column_count = gate_base_weight.shape[1]
    doubled_rank = adapter_down_maps.shape[2]
    adapter_rank_width = doubled_rank // 2
    gathered = lax.all_gather(tokens, "gy", axis=0, tiled=True)
    summed = lax.psum_scatter(
        jnp.concatenate(
            [
                jnp.dot(gathered, gate_base_weight, preferred_element_type=jnp.float32),
                jnp.dot(gathered, up_base_weight, preferred_element_type=jnp.float32),
            ],
            axis=1,
        ).astype(jnp.bfloat16),
        "gx",
        scatter_dimension=0,
        tiled=True,
    ).astype(jnp.float32)
    slot_all = jnp.sum(
        jnp.where(tenant == lax.iota(jnp.int32, tenants)[None, :], tenant_slot_index[None, :], 0),
        axis=1,
    )
    onehot = (slot_all[:, None] == lax.iota(jnp.int32, devices)[None, :]).astype(jnp.int32)
    blocked = onehot.reshape(tile_grid_rows, block, devices)
    before = jnp.cumsum(blocked, axis=1) - blocked
    position = jnp.sum(before * blocked, axis=2).reshape(total_rows)
    send_slot = lax.dynamic_slice_in_dim(slot_all, row_gy * local_rows, local_rows)
    send_rank = lax.dynamic_slice_in_dim(position, row_gy * local_rows, local_rows)
    target = (send_slot * groups + lax.iota(jnp.int32, local_rows) // block) * CAP + send_rank
    outgoing = jnp.zeros((devices * groups * CAP, tile_width), jnp.bfloat16).at[target].set(tokens)
    arrived = lax.all_to_all(
        outgoing.reshape(devices, groups * CAP, tile_width),
        ("gx", "gy"),
        split_axis=0,
        concat_axis=0,
        tiled=True,
    )
    arrived = arrived.reshape(tile_grid_rows, tile_grid_columns * groups * CAP, tile_width)
    down_local = adapter_down_maps[0].reshape(tile_grid_rows, tile_width, doubled_rank)
    low = jnp.einsum("isk,ikr->sr", arrived, down_local, preferred_element_type=jnp.float32).astype(
        jnp.bfloat16
    )
    low = low.reshape(tile_grid_rows, CAP, doubled_rank)
    gate_up_map = adapter_up_maps[0, :adapter_rank_width].reshape(
        adapter_rank_width, tile_grid_columns, column_count
    )
    up_up_map = adapter_up_maps[0, adapter_rank_width:].reshape(
        adapter_rank_width, tile_grid_columns, column_count
    )
    delta_gate = jnp.einsum(
        "gcr,rjf->gjcf",
        low[:, :, :adapter_rank_width],
        gate_up_map,
        preferred_element_type=jnp.float32,
    ).astype(jnp.bfloat16)
    delta_up = jnp.einsum(
        "gcr,rjf->gjcf",
        low[:, :, adapter_rank_width:],
        up_up_map,
        preferred_element_type=jnp.float32,
    ).astype(jnp.bfloat16)
    back_gate, back_up = (
        lax.all_to_all(
            delta_gate.reshape(devices, CAP, column_count),
            ("gx", "gy"),
            split_axis=0,
            concat_axis=0,
            tiled=True,
        ),
        lax.all_to_all(
            delta_up.reshape(devices, CAP, column_count),
            ("gx", "gy"),
            split_axis=0,
            concat_axis=0,
            tiled=True,
        ),
    )
    back_gate = back_gate.reshape(devices * CAP, column_count)
    back_up = back_up.reshape(devices * CAP, column_count)
    own_slot = lax.dynamic_slice_in_dim(slot_all, row_gx * block, block)
    own_rank = lax.dynamic_slice_in_dim(position, row_gx * block, block)
    pick = own_slot * CAP + own_rank
    gate_value = summed[:, :column_count] + back_gate[pick].astype(jnp.float32)
    up_value = summed[:, column_count:] + back_up[pick].astype(jnp.float32)
    return (jax.nn.silu(gate_value) * up_value).astype(jnp.bfloat16)


def solution(mesh):
    return jax.shard_map(
        body,
        mesh=mesh,
        in_specs=(
            P("gy", "gx"),
            P("gx", "gy"),
            P("gx", "gy"),
            P(("gx", "gy"), None, None),
            P(("gx", "gy"), None, None),
            P(),
            P(),
        ),
        out_specs=P("gx", "gy"),
        check_vma=False,
    )
```

profile of v0, /device:TPU:1, one launch (start us, length us, event | category | flops | bytes accessed | tf_op | source)
XLA Modules:
  0.0 404.3 jit_solution(10806545864353587675)
XLA Ops:
  6.5 0.0 copy-start
  6.5 0.0 all-gather.2.cloned.1.call-start
  6.5 0.7 all-gather.2.cloned.1.call-update
  7.3 0.0 reduce-scatter.4.cloned.1.call-start
  7.3 30.6 %all-gather.2.cloned.1.call-done = bf16[2048,512]{1,0:T(8,128)(2,1)} async-done(((bf16[256,512]{1,0:T(8,128)(2,1)}), bf16[2048,512]{1,0:T(8,128)(2,1)}) %all-gather.2.cloned.1.call-update) | async-done | bytes 2097168 | tf_op jit(solution)/shard_map/all_gather | solution.py:32
  37.9 13.8 %convolution_convert_fusion = bf16[2048,3696]{0,1:T(8,128)(2,1)} fusion(bf16[2048,512]{1,0:T(8,128)(2,1)} %all-gather.2.cloned.1.call-done, bf16[512,3696]{0,1:T(8,128)(2,1)} %param.9), kind=kOutput, calls=%fused_computation.4 | convolution fusion | flops 7758643200 | bytes 21020672 | tf_op jit(solution)/shard_map/dot_general | solution.py:37
  51.8 0.0 copy-done.5
  51.8 0.0 copy-done.6
  51.8 10.8 %convolution_convert_fusion.1 = bf16[2048,3696]{0,1:T(8,128)(2,1)} fusion(bf16[2048,512]{1,0:T(8,128)(2,1)S(1)} %copy-done.6, bf16[512,3696]{0,1:T(8,128)(2,1)S(1)} %copy-done.5), kind=kOutput, calls=%fused_computation.5 | convolution fusion | flops 7758643200 | bytes 21020672 | tf_op jit(solution)/shard_map/dot_general | solution.py:36
  62.6 21.4 %pad_maximum_fusion = bf16[2048,7392]{0,1:T(8,128)(2,1)} fusion(bf16[2048,3696]{0,1:T(8,128)(2,1)} %convolution_convert_fusion, bf16[2048,3696]{0,1:T(8,128)(2,1)} %convolution_convert_fusion.1), kind=kLoop, calls=%fused_computation.3 | loop fusion | flops 60555264 | bytes 60555264 | tf_op jit(solution)/shard_map/concatenate | solution.py:34
  84.0 36.5 %copy.60 = bf16[2048,7392]{1,0:T(8,128)(2,1)} copy(bf16[2048,7392]{0,1:T(8,128)(2,1)} %pad_maximum_fusion) | data formatting | bytes 60555264
  120.5 0.0 reduce-scatter.4.cloned.1.call-update
  120.5 0.7 copy-done.3
  121.2 0.0 copy-done.4
  121.2 0.6 select_reduce_fusion.1
  121.8 0.1 copy.47
  121.9 2.8 select_reduce_fusion
  124.7 0.1 copy.48
  124.8 0.1 compare_select_fusion
  124.9 3.1 scatter_custom_fusion
  127.9 8.1 %all-to-all-start = ((bf16[128,8,512]{2,1,0:T(8,128)(2,1)}), bf16[128,8,512]{2,1,0:T(8,128)(2,1)S(1)}, u32[]{:S(2)}, u32[]{:S(2)}) async-start(bf16[128,8,512]{2,1,0:T(8,128)(2,1)} %bitcast.48), calls=%async_computation | async-start | bytes 2097152 | tf_op jit(solution)/shard_map/all_to_all | solution.py:57
  136.1 5.6 %fusion.19 = (bf16[1,64,29568]{2,1,0:T(8,128)(2,1)}, bf16[1,64,29568]{2,1,0:T(8,128)(2,1)}) fusion(bf16[1,128,29568]{2,1,0:T(8,128)(2,1)} %param.11), kind=kLoop, calls=%fused_computation.44 | loop fusion | bytes 15138816 | tf_op jit(solution)/shard_map/slice | solution.py:70
  141.7 7.5 %reshape_squeeze.11 = bf16[64,8,3696]{2,1,0:T(8,128)(2,1)} reshape(bf16[1,64,29568]{2,1,0:T(8,128)(2,1)} %get-tuple-element.6) | data formatting | bytes 7569408 | tf_op jit(solution)/shard_map/reshape;squeeze | solution.py:73
  149.2 17.1 %all-to-all-done = bf16[128,8,512]{2,1,0:T(8,128)(2,1)S(1)} async-done(((bf16[128,8,512]{2,1,0:T(8,128)(2,1)}), bf16[128,8,512]{2,1,0:T(8,128)(2,1)S(1)}, u32[]{:S(2)}, u32[]{:S(2)}) %all-to-all-start) | async-done | bytes 1048608 | tf_op jit(solution)/shard_map/all_to_all | solution.py:57
  166.3 0.0 copy-done
  166.3 0.5 fusion.12
  166.8 0.1 fusion.20
  166.9 3.3 fusion.1
  170.2 0.6 copy.78
  170.9 4.9 %copy.56 = bf16[128,4,3696]{2,1,0:T(4,128)(2,1)} copy(bf16[128,4,3696]{2,0,1:T(8,128)(2,1)S(1)} %bitcast.45) | data formatting | bytes 7569408 | tf_op jit(solution)/shard_map/reshape | solution.py:97
  175.8 6.1 %all-to-all-start.2 = ((bf16[128,4,3696]{2,1,0:T(4,128)(2,1)}), bf16[128,4,3696]{2,1,0:T(4,128)(2,1)}, u32[]{:S(2)}, u32[]{:S(2)}) async-start(bf16[128,4,3696]{2,1,0:T(4,128)(2,1)} %copy.56), calls=%async_computation.2 | async-start | bytes 7602176 | tf_op jit(solution)/shard_map/all_to_all | solution.py:96
  181.9 7.5 %reshape_squeeze.10 = bf16[64,8,3696]{2,1,0:T(8,128)(2,1)} reshape(bf16[1,64,29568]{2,1,0:T(8,128)(2,1)} %get-tuple-element.5) | data formatting | bytes 7569408 | tf_op jit(solution)/shard_map/reshape;squeeze | solution.py:70
  189.4 3.2 fusion
  192.6 0.6 copy.79
  193.3 4.8 %copy.52 = bf16[128,4,3696]{2,1,0:T(4,128)(2,1)} copy(bf16[128,4,3696]{2,0,1:T(8,128)(2,1)S(1)} %bitcast.46) | data formatting | bytes 7569408 | tf_op jit(solution)/shard_map/reshape | solution.py:90
  198.0 65.6 %all-to-all-done.2 = bf16[128,4,3696]{2,1,0:T(4,128)(2,1)} async-done(((bf16[128,4,3696]{2,1,0:T(4,128)(2,1)}), bf16[128,4,3696]{2,1,0:T(4,128)(2,1)}, u32[]{:S(2)}, u32[]{:S(2)}) %all-to-all-start.2) | async-done | bytes 3784736 | tf_op jit(solution)/shard_map/all_to_all | solution.py:96
  263.6 6.3 %all-to-all-start.1 = ((bf16[128,4,3696]{2,1,0:T(4,128)(2,1)}), bf16[128,4,3696]{2,1,0:T(4,128)(2,1)}, u32[]{:S(2)}, u32[]{:S(2)}) async-start(bf16[128,4,3696]{2,1,0:T(4,128)(2,1)} %copy.52), calls=%async_computation.1 | async-start | bytes 7602176 | tf_op jit(solution)/shard_map/all_to_all | solution.py:89
  269.9 0.1 compare_select_fusion.1
  270.0 7.2 %reshape.42 = bf16[512,3696]{1,0:T(8,128)(2,1)} reshape(bf16[128,4,3696]{2,1,0:T(4,128)(2,1)} %all-to-all-done.2) | data formatting | bytes 7569408 | tf_op jit(solution)/shard_map/reshape | solution.py:105
  277.2 5.8 %gather_fusion.1 = bf16[128,3696]{1,0:T(8,128)(2,1)} fusion(bf16[512,3696]{1,0:T(8,128)(2,1)} %reshape.42, s32[1024]{0:T(1024)S(1)} %pad_clamp_fusion), kind=kCustom, calls=%fused_computation.1 | custom fusion | bytes 1892864 | tf_op jit(solution)/shard_map/gather | solution.py:110
  283.0 68.3 %all-to-all-done.1 = bf16[128,4,3696]{2,1,0:T(4,128)(2,1)} async-done(((bf16[128,4,3696]{2,1,0:T(4,128)(2,1)}), bf16[128,4,3696]{2,1,0:T(4,128)(2,1)}, u32[]{:S(2)}, u32[]{:S(2)}) %all-to-all-start.1) | async-done | bytes 3784736 | tf_op jit(solution)/shard_map/all_to_all | solution.py:89
  351.3 7.0 %reshape.40 = bf16[512,3696]{1,0:T(8,128)(2,1)} reshape(bf16[128,4,3696]{2,1,0:T(4,128)(2,1)} %all-to-all-done.1) | data formatting | bytes 7569408 | tf_op jit(solution)/shard_map/reshape | solution.py:104
  358.3 5.9 %gather_fusion = bf16[128,3696]{1,0:T(8,128)(2,1)} fusion(bf16[512,3696]{1,0:T(8,128)(2,1)} %reshape.40, s32[1024]{0:T(1024)S(1)} %pad_clamp_fusion), kind=kCustom, calls=%fused_computation | custom fusion | bytes 1892864 | tf_op jit(solution)/shard_map/gather | solution.py:109
  364.2 29.1 %reduce-scatter.4.cloned.1.call-done = bf16[128,7392]{1,0:T(8,128)(2,1)} async-done(((bf16[2048,7392]{1,0:T(8,128)(2,1)}), bf16[128,7392]{1,0:T(8,128)(2,1)}) %reduce-scatter.4.cloned.1.call-update) | async-done | bytes 1892368 | tf_op jit(solution)/shard_map/reduce_scatter | solution.py:33
  393.3 1.9 convert_element_type.32
  395.2 0.1 copy-done.2
  395.3 0.8 fusion.7
  396.1 1.3 copy.57
  (8 shorter events, 0.0 us)
Async XLA Ops:
  6.5 159.8 %copy-start = (bf16[1,8192,128]{2,1,0:T(8,128)(2,1)S(1)}, bf16[1,8192,128]{2,1,0:T(8,128)(2,1)}, u32[]{:S(2)}) copy-start(bf16[1,8192,128]{2,1,0:T(8,128)(2,1)} %param.10) | copy-start | bytes 6291460
  6.5 31.4 %all-gather.2.cloned.1.call-start = ((), (), s32[]{:S(2)}) async-start(), calls=%async_computation.4 | async-start | bytes 2359296 | tf_op jit(solution)/shard_map/all_gather | solution.py:32
  7.3 386.0 %reduce-scatter.4.cloned.1.call-start = ((), (), s32[]{:S(2)}) async-start(), calls=%async_computation.5 | async-start | bytes 32309248 | tf_op jit(solution)/shard_map/reduce_scatter | solution.py:33
  37.9 13.8 %copy-start.5 = (bf16[512,3696]{0,1:T(8,128)(2,1)S(1)}, bf16[512,3696]{0,1:T(8,128)(2,1)}, u32[]{:S(2)}) copy-start(bf16[512,3696]{0,1:T(8,128)(2,1)} %param.8) | copy-start | bytes 11354116
  37.9 13.8 %copy-start.6 = (bf16[2048,512]{1,0:T(8,128)(2,1)S(1)}, bf16[2048,512]{1,0:T(8,128)(2,1)}, u32[]{:S(2)}) copy-start(bf16[2048,512]{1,0:T(8,128)(2,1)} %all-gather.2.cloned.1.call-done) | copy-start | bytes 6291460
  120.5 0.7 copy-start.3
  120.5 0.7 copy-start.4
  127.9 38.4 %all-to-all-start = ((bf16[128,8,512]{2,1,0:T(8,128)(2,1)}), bf16[128,8,512]{2,1,0:T(8,128)(2,1)S(1)}, u32[]{:S(2)}, u32[]{:S(2)}) async-start(bf16[128,8,512]{2,1,0:T(8,128)(2,1)} %bitcast.48), calls=%async_computation | async-start | bytes 2097152 | tf_op jit(solution)/shard_map/all_to_all | solution.py:57
  175.8 87.8 %all-to-all-start.2 = ((bf16[128,4,3696]{2,1,0:T(4,128)(2,1)}), bf16[128,4,3696]{2,1,0:T(4,128)(2,1)}, u32[]{:S(2)}, u32[]{:S(2)}) async-start(bf16[128,4,3696]{2,1,0:T(4,128)(2,1)} %copy.56), calls=%async_computation.2 | async-start | bytes 7602176 | tf_op jit(solution)/shard_map/all_to_all | solution.py:96
  263.6 87.7 %all-to-all-start.1 = ((bf16[128,4,3696]{2,1,0:T(4,128)(2,1)}), bf16[128,4,3696]{2,1,0:T(4,128)(2,1)}, u32[]{:S(2)}, u32[]{:S(2)}) async-start(bf16[128,4,3696]{2,1,0:T(4,128)(2,1)} %copy.52), calls=%async_computation.1 | async-start | bytes 7602176 | tf_op jit(solution)/shard_map/all_to_all | solution.py:89
  393.3 1.9 copy-start.1
  393.3 2.0 copy-start.2
Sparse Core Ops, SparseCore 0:
  9.1 28.7 all-gather.1
  120.6 272.5 reduce-scatter.3
where the time goes:
time: 406 us; the launch traced here: 404 us
  waiting for transfers between devices  211 us (52%)
  local copies, waits for them, and re-layouts  99.4 us (24%)
  matrix products  31.7 us (8%)
  other arithmetic  27.8 us (7%)
  starting transfers between devices  20.6 us (5%)
  between operations  13.5 us (3%)
    all_to_all x1, waiting for transfers between devices, body(): lax.all_to_all(delta_gate.reshape(devices, CAP, column_count), ('gx', 'gy...  68.3 us
    all_to_all x1, waiting for transfers between devices, body(): lax.all_to_all(delta_up.reshape(devices, CAP, column_count), ('gx', 'gy')...  65.6 us
    unnamed x15, local copies, waits for them, and re-layouts  37.3 us
    all_gather x1, waiting for transfers between devices, body(): gathered = lax.all_gather(tokens, 'gy', axis=0, tiled=True)  30.6 us
    reduce_scatter x1, waiting for transfers between devices, body(): lax.psum_scatter(jnp.concatenate([jnp.dot(gathered, gate_base_weight, pre...  29.1 us
    concatenate x1, other arithmetic, body(): jnp.concatenate([jnp.dot(gathered, gate_base_weight, preferred_element_ty...  21.4 us
    all_to_all x1, waiting for transfers between devices, body(): lax.all_to_all(outgoing.reshape(devices, groups * CAP, tile_width), ('gx'...  17.1 us
    dot_general x1, matrix products, body(): jnp.dot(gathered, up_base_weight, preferred_element_type=jnp.float32)  13.8 us
  transfers between devices with their start and end apart: 5, of which 5 were waited for; matrix products, arithmetic and copies ran while one was open for 18% of the time, Pallas kernels for 0%

commit v1 on v0

--- a/solution.py
+++ b/solution.py
@@ -2,6 +2,7 @@
 import jax.numpy as jnp
 from jax import lax
 from jax.sharding import PartitionSpec as P
+from jax.experimental.layout import Layout, with_layout_constraint
 
 CAP = 4
 
@@ -30,18 +31,12 @@
     doubled_rank = adapter_down_maps.shape[2]
     adapter_rank_width = doubled_rank // 2
     gathered = lax.all_gather(tokens, "gy", axis=0, tiled=True)
-    summed = lax.psum_scatter(
-        jnp.concatenate(
-            [
-                jnp.dot(gathered, gate_base_weight, preferred_element_type=jnp.float32),
-                jnp.dot(gathered, up_base_weight, preferred_element_type=jnp.float32),
-            ],
-            axis=1,
-        ).astype(jnp.bfloat16),
-        "gx",
-        scatter_dimension=0,
-        tiled=True,
-    ).astype(jnp.float32)
+    gate_sum = lax.psum_scatter(
+        with_layout_constraint(jnp.dot(gathered, gate_base_weight, preferred_element_type=jnp.float32).astype(jnp.bfloat16), Layout(major_to_minor=(0, 1))),
+        "gx", scatter_dimension=0, tiled=True).astype(jnp.float32)
+    up_sum = lax.psum_scatter(
+        with_layout_constraint(jnp.dot(gathered, up_base_weight, preferred_element_type=jnp.float32).astype(jnp.bfloat16), Layout(major_to_minor=(0, 1))),
+        "gx", scatter_dimension=0, tiled=True).astype(jnp.float32)
     slot_all = jnp.sum(
         jnp.where(tenant == lax.iota(jnp.int32, tenants)[None, :], tenant_slot_index[None, :], 0),
         axis=1,
@@ -106,8 +101,8 @@
     own_slot = lax.dynamic_slice_in_dim(slot_all, row_gx * block, block)
     own_rank = lax.dynamic_slice_in_dim(position, row_gx * block, block)
     pick = own_slot * CAP + own_rank
-    gate_value = summed[:, :column_count] + back_gate[pick].astype(jnp.float32)
-    up_value = summed[:, column_count:] + back_up[pick].astype(jnp.float32)
+    gate_value = gate_sum + back_gate[pick].astype(jnp.float32)
+    up_value = up_sum + back_up[pick].astype(jnp.float32)
     return (jax.nn.silu(gate_value) * up_value).astype(jnp.bfloat16)
 
 

time: 406 us -> 365 us (0.90)
  local copies, waits for them, and re-layouts: 99.4 us -> 62.1 us
  other arithmetic: 27.8 us -> 6.42 us
  waiting for transfers between devices: 211 us -> 228 us
    reduce_scatter x1 -> x2, waiting for transfers between devices: 29.1 us -> 90.7 us  [the longest x1 90.7 us: body(): lax.psum_scatter(with_layout_constraint(jnp.dot(gathered, gate_base_weigh...]
    unnamed x15 -> x6, local copies, waits for them, and re-layouts: 37.3 us -> 0.67 us
    all_to_all x1, waiting for transfers between devices: 68.3 us -> 39.1 us  [body(): lax.all_to_all(delta_gate.reshape(devices, CAP, column_count), ('gx', 'gy...]
    concatenate x1 -> x0, other arithmetic: 21.4 us -> none  [body(): jnp.concatenate([jnp.dot(gathered, gate_base_weight, preferred_element_ty...]
    all_to_all x1, waiting for transfers between devices: 65.6 us -> 49.8 us  [body(): lax.all_to_all(delta_up.reshape(devices, CAP, column_count), ('gx', 'gy')...]
  transfers between devices with their start and end apart: 5 -> 6, of which waited for: 5 -> 5; matrix products, arithmetic and copies ran while one was open for 18% -> 23% of each run, Pallas kernels for 0% -> 0%
where the time goes in v1:
time: 365 us; the launch traced here: 364 us
  waiting for transfers between devices  228 us (62%)
  local copies, waits for them, and re-layouts  62.1 us (17%)
  matrix products  35.1 us (10%)
  starting transfers between devices  19.1 us (5%)
  between operations  13.2 us (4%)
  other arithmetic  6.42 us (2%)
    reduce_scatter x1, waiting for transfers between devices, body(): lax.psum_scatter(with_layout_constraint(jnp.dot(gathered, gate_base_weigh...  90.7 us
    all_to_all x1, waiting for transfers between devices, body(): lax.all_to_all(delta_up.reshape(devices, CAP, column_count), ('gx', 'gy')...  49.8 us
    all_to_all x1, waiting for transfers between devices, body(): lax.all_to_all(delta_gate.reshape(devices, CAP, column_count), ('gx', 'gy...  39.1 us
    all_gather x1, waiting for transfers between devices, body(): gathered = lax.all_gather(tokens, 'gy', axis=0, tiled=True)  30.6 us
    all_to_all x1, waiting for transfers between devices, body(): lax.all_to_all(outgoing.reshape(devices, groups * CAP, tile_width), ('gx'...  17.3 us
    dot_general x1, matrix products, body(): jnp.dot(gathered, gate_base_weight, preferred_element_type=jnp.float32)  14.1 us
    dot_general x1, matrix products, body(): jnp.dot(gathered, up_base_weight, preferred_element_type=jnp.float32)  14 us
    all_to_all x1, starting transfers between devices, body(): lax.all_to_all(outgoing.reshape(devices, groups * CAP, tile_width), ('gx'...  8.15 us
  transfers between devices with their start and end apart: 6, of which 5 were waited for; matrix products, arithmetic and copies ran while one was open for 23% of the time, Pallas kernels for 0%

profile of v1, /device:TPU:1, one launch (start us, length us, event | category | flops | bytes accessed | tf_op | source)
XLA Modules:
  0.0 364.2 jit_solution(4737245542923288440)
XLA Ops:
  6.5 0.0 copy-start
  6.5 0.0 all-gather.2.cloned.1.call-start
  6.5 0.7 all-gather.2.cloned.1.call-update
  7.3 0.0 reduce-scatter.5.cloned.1.call-start
  7.3 30.6 %all-gather.2.cloned.1.call-done = bf16[2048,512]{1,0:T(8,128)(2,1)} async-done(((bf16[256,512]{1,0:T(8,128)(2,1)}), bf16[2048,512]{1,0:T(8,128)(2,1)}) %all-gather.2.cloned.1.call-update) | async-done | bytes 2097168 | tf_op jit(solution)/shard_map/all_gather | solution.py:33
  37.9 14.0 %convolution_convert_fusion = bf16[2048,3696]{1,0:T(8,128)(2,1)} fusion(bf16[2048,512]{1,0:T(8,128)(2,1)} %all-gather.2.cloned.1.call-done, bf16[512,3696]{0,1:T(8,128)(2,1)} %param.9), kind=kOutput, calls=%fused_computation.3 | convolution fusion | flops 7758643200 | bytes 21020672 | tf_op jit(solution)/shard_map/dot_general | solution.py:38
  51.9 0.0 reduce-scatter.5.cloned.1.call-update
  51.9 0.0 reduce-scatter.3.cloned.1.call-start
  52.0 14.1 %convolution_convert_fusion.1 = bf16[2048,3696]{1,0:T(8,128)(2,1)} fusion(bf16[2048,512]{1,0:T(8,128)(2,1)} %all-gather.2.cloned.1.call-done, bf16[512,3696]{0,1:T(8,128)(2,1)} %param.8), kind=kOutput, calls=%fused_computation.4 | convolution fusion | flops 7758643200 | bytes 21020672 | tf_op jit(solution)/shard_map/dot_general | solution.py:35
  66.1 0.0 copy-start.1
  66.1 0.0 copy-start.2
  66.1 0.0 reduce-scatter.3.cloned.1.call-update
  66.1 0.7 copy-done.1
  66.8 0.0 copy-done.2
  66.8 0.6 select_reduce_fusion.1
  67.4 0.1 copy.42
  67.5 2.8 select_reduce_fusion
  70.3 0.1 copy.43
  70.3 0.1 compare_select_fusion
  70.4 3.1 scatter_custom_fusion
  73.5 8.2 %all-to-all-start = ((bf16[128,8,512]{2,1,0:T(8,128)(2,1)}), bf16[128,8,512]{2,1,0:T(8,128)(2,1)S(1)}, u32[]{:S(2)}, u32[]{:S(2)}) async-start(bf16[128,8,512]{2,1,0:T(8,128)(2,1)} %bitcast.48), calls=%async_computation.1 | async-start | bytes 2097152 | tf_op jit(solution)/shard_map/all_to_all | solution.py:52
  81.6 5.5 %fusion.17 = (bf16[1,64,29568]{2,1,0:T(8,128)(2,1)}, bf16[1,64,29568]{2,1,0:T(8,128)(2,1)}) fusion(bf16[1,128,29568]{2,1,0:T(8,128)(2,1)} %param.11), kind=kLoop, calls=%fused_computation.40 | loop fusion | bytes 15138816 | tf_op jit(solution)/shard_map/slice | solution.py:65
  87.1 7.5 %reshape_squeeze.10 = bf16[64,8,3696]{2,1,0:T(8,128)(2,1)} reshape(bf16[1,64,29568]{2,1,0:T(8,128)(2,1)} %get-tuple-element.5) | data formatting | bytes 7569408 | tf_op jit(solution)/shard_map/reshape;squeeze | solution.py:65
  94.7 17.3 %all-to-all-done = bf16[128,8,512]{2,1,0:T(8,128)(2,1)S(1)} async-done(((bf16[128,8,512]{2,1,0:T(8,128)(2,1)}), bf16[128,8,512]{2,1,0:T(8,128)(2,1)S(1)}, u32[]{:S(2)}, u32[]{:S(2)}) %all-to-all-start) | async-done | bytes 1048608 | tf_op jit(solution)/shard_map/all_to_all | solution.py:52
  111.9 0.0 copy-done
  111.9 0.5 fusion.10
  112.5 0.1 fusion.18
  112.5 3.3 fusion
  115.9 0.6 copy.72
  116.5 4.9 %copy.47 = bf16[128,4,3696]{2,1,0:T(4,128)(2,1)} copy(bf16[128,4,3696]{2,0,1:T(8,128)(2,1)S(1)} %bitcast.45) | data formatting | bytes 7569408 | tf_op jit(solution)/shard_map/reshape | solution.py:85
  121.4 5.7 %all-to-all-start.1 = ((bf16[128,4,3696]{2,1,0:T(4,128)(2,1)}), bf16[128,4,3696]{2,1,0:T(4,128)(2,1)}, u32[]{:S(2)}, u32[]{:S(2)}) async-start(bf16[128,4,3696]{2,1,0:T(4,128)(2,1)} %copy.47), calls=%async_computation.2 | async-start | bytes 7602176 | tf_op jit(solution)/shard_map/all_to_all | solution.py:84
  127.1 7.6 %reshape_squeeze.11 = bf16[64,8,3696]{2,1,0:T(8,128)(2,1)} reshape(bf16[1,64,29568]{2,1,0:T(8,128)(2,1)} %get-tuple-element.6) | data formatting | bytes 7569408 | tf_op jit(solution)/shard_map/reshape;squeeze | solution.py:68
  134.6 3.3 fusion.1
  137.9 0.6 copy.71
  138.5 4.8 %copy.51 = bf16[128,4,3696]{2,1,0:T(4,128)(2,1)} copy(bf16[128,4,3696]{2,0,1:T(8,128)(2,1)S(1)} %bitcast.46) | data formatting | bytes 7569408 | tf_op jit(solution)/shard_map/reshape | solution.py:92
  143.3 39.1 %all-to-all-done.1 = bf16[128,4,3696]{2,1,0:T(4,128)(2,1)} async-done(((bf16[128,4,3696]{2,1,0:T(4,128)(2,1)}), bf16[128,4,3696]{2,1,0:T(4,128)(2,1)}, u32[]{:S(2)}, u32[]{:S(2)}) %all-to-all-start.1) | async-done | bytes 3784736 | tf_op jit(solution)/shard_map/all_to_all | solution.py:84
  182.4 5.2 %all-to-all-start.2 = ((bf16[128,4,3696]{2,1,0:T(4,128)(2,1)}), bf16[128,4,3696]{2,1,0:T(4,128)(2,1)}, u32[]{:S(2)}, u32[]{:S(2)}) async-start(bf16[128,4,3696]{2,1,0:T(4,128)(2,1)} %copy.51), calls=%async_computation.4 | async-start | bytes 7602176 | tf_op jit(solution)/shard_map/all_to_all | solution.py:91
  187.6 0.1 compare_select_fusion.1
  187.7 7.0 %reshape.40 = bf16[512,3696]{1,0:T(8,128)(2,1)} reshape(bf16[128,4,3696]{2,1,0:T(4,128)(2,1)} %all-to-all-done.1) | data formatting | bytes 7569408 | tf_op jit(solution)/shard_map/reshape | solution.py:99
  194.8 5.6 %gather_fusion = bf16[128,3696]{1,0:T(8,128)(2,1)} fusion(bf16[512,3696]{1,0:T(8,128)(2,1)} %reshape.40, s32[1024]{0:T(1024)S(1)} %pad_clamp_fusion), kind=kCustom, calls=%fused_computation | custom fusion | bytes 1892864 | tf_op jit(solution)/shard_map/gather | solution.py:104
  200.4 49.8 %all-to-all-done.2 = bf16[128,4,3696]{2,1,0:T(4,128)(2,1)} async-done(((bf16[128,4,3696]{2,1,0:T(4,128)(2,1)}), bf16[128,4,3696]{2,1,0:T(4,128)(2,1)}, u32[]{:S(2)}, u32[]{:S(2)}) %all-to-all-start.2) | async-done | bytes 3784736 | tf_op jit(solution)/shard_map/all_to_all | solution.py:91
  250.2 7.0 %reshape.42 = bf16[512,3696]{1,0:T(8,128)(2,1)} reshape(bf16[128,4,3696]{2,1,0:T(4,128)(2,1)} %all-to-all-done.2) | data formatting | bytes 7569408 | tf_op jit(solution)/shard_map/reshape | solution.py:100
  257.2 5.6 %gather_fusion.1 = bf16[128,3696]{1,0:T(8,128)(2,1)} fusion(bf16[512,3696]{1,0:T(8,128)(2,1)} %reshape.42, s32[1024]{0:T(1024)S(1)} %pad_clamp_fusion), kind=kCustom, calls=%fused_computation.1 | custom fusion | bytes 1892864 | tf_op jit(solution)/shard_map/gather | solution.py:105
  262.8 0.0 reduce-scatter.5.cloned.1.call-done
  262.8 90.7 %reduce-scatter.3.cloned.1.call-done = bf16[128,3696]{1,0:T(8,128)(2,1)} async-done(((bf16[2048,3696]{1,0:T(8,128)(2,1)}), bf16[128,3696]{1,0:T(8,128)(2,1)}) %reduce-scatter.3.cloned.1.call-update) | async-done | bytes 946192 | tf_op jit(solution)/shard_map/reduce_scatter | solution.py:34
  353.5 2.8 multiply_convert_fusion
  356.3 1.3 copy.52
  (1 shorter events, 0.0 us)
Async XLA Ops:
  6.5 105.4 %copy-start = (bf16[1,8192,128]{2,1,0:T(8,128)(2,1)S(1)}, bf16[1,8192,128]{2,1,0:T(8,128)(2,1)}, u32[]{:S(2)}) copy-start(bf16[1,8192,128]{2,1,0:T(8,128)(2,1)} %param.10) | copy-start | bytes 6291460
  6.5 31.4 %all-gather.2.cloned.1.call-start = ((), (), s32[]{:S(2)}) async-start(), calls=%async_computation.5 | async-start | bytes 2359296 | tf_op jit(solution)/shard_map/all_gather | solution.py:33
  7.3 255.6 %reduce-scatter.5.cloned.1.call-start = ((), (), s32[]{:S(2)}) async-start(), calls=%async_computation.7 | async-start | bytes 16154624 | tf_op jit(solution)/shard_map/reduce_scatter | solution.py:37
  51.9 301.6 %reduce-scatter.3.cloned.1.call-start = ((), (), s32[]{:S(2)}) async-start(), calls=%async_computation.6 | async-start | bytes 16154624 | tf_op jit(solution)/shard_map/reduce_scatter | solution.py:34
  66.1 0.7 copy-start.1
  66.1 0.7 copy-start.2
  73.5 38.5 %all-to-all-start = ((bf16[128,8,512]{2,1,0:T(8,128)(2,1)}), bf16[128,8,512]{2,1,0:T(8,128)(2,1)S(1)}, u32[]{:S(2)}, u32[]{:S(2)}) async-start(bf16[128,8,512]{2,1,0:T(8,128)(2,1)} %bitcast.48), calls=%async_computation.1 | async-start | bytes 2097152 | tf_op jit(solution)/shard_map/all_to_all | solution.py:52
  121.4 61.0 %all-to-all-start.1 = ((bf16[128,4,3696]{2,1,0:T(4,128)(2,1)}), bf16[128,4,3696]{2,1,0:T(4,128)(2,1)}, u32[]{:S(2)}, u32[]{:S(2)}) async-start(bf16[128,4,3696]{2,1,0:T(4,128)(2,1)} %copy.47), calls=%async_computation.2 | async-start | bytes 7602176 | tf_op jit(solution)/shard_map/all_to_all | solution.py:84
  182.4 67.8 %all-to-all-start.2 = ((bf16[128,4,3696]{2,1,0:T(4,128)(2,1)}), bf16[128,4,3696]{2,1,0:T(4,128)(2,1)}, u32[]{:S(2)}, u32[]{:S(2)}) async-start(bf16[128,4,3696]{2,1,0:T(4,128)(2,1)} %copy.51), calls=%async_computation.4 | async-start | bytes 7602176 | tf_op jit(solution)/shard_map/all_to_all | solution.py:91
Sparse Core Ops, SparseCore 0:
  9.1 28.7 all-gather.1
  52.1 191.3 reduce-scatter.4
  247.3 106.1 reduce-scatter.2

commit v2 on v1

--- a/solution.py
+++ b/solution.py
@@ -31,12 +31,12 @@
     doubled_rank = adapter_down_maps.shape[2]
     adapter_rank_width = doubled_rank // 2
     gathered = lax.all_gather(tokens, "gy", axis=0, tiled=True)
-    gate_sum = lax.psum_scatter(
-        with_layout_constraint(jnp.dot(gathered, gate_base_weight, preferred_element_type=jnp.float32).astype(jnp.bfloat16), Layout(major_to_minor=(0, 1))),
-        "gx", scatter_dimension=0, tiled=True).astype(jnp.float32)
-    up_sum = lax.psum_scatter(
-        with_layout_constraint(jnp.dot(gathered, up_base_weight, preferred_element_type=jnp.float32).astype(jnp.bfloat16), Layout(major_to_minor=(0, 1))),
-        "gx", scatter_dimension=0, tiled=True).astype(jnp.float32)
+    both_weights = jnp.concatenate([gate_base_weight, up_base_weight], axis=1)
+    partial = with_layout_constraint(
+        jnp.dot(gathered, both_weights, preferred_element_type=jnp.float32).astype(jnp.bfloat16),
+        Layout(major_to_minor=(0, 1)),
+    )
+    summed = lax.psum_scatter(partial, "gx", scatter_dimension=0, tiled=True)
     slot_all = jnp.sum(
         jnp.where(tenant == lax.iota(jnp.int32, tenants)[None, :], tenant_slot_index[None, :], 0),
         axis=1,
@@ -80,29 +80,19 @@
         up_up_map,
         preferred_element_type=jnp.float32,
     ).astype(jnp.bfloat16)
-    back_gate, back_up = (
-        lax.all_to_all(
-            delta_gate.reshape(devices, CAP, column_count),
-            ("gx", "gy"),
-            split_axis=0,
-            concat_axis=0,
-            tiled=True,
-        ),
-        lax.all_to_all(
-            delta_up.reshape(devices, CAP, column_count),
-            ("gx", "gy"),
-            split_axis=0,
-            concat_axis=0,
-            tiled=True,
-        ),
+    delta = jnp.concatenate(
+        [delta_gate.reshape(devices, CAP, column_count), delta_up.reshape(devices, CAP, column_count)], axis=2
     )
-    back_gate = back_gate.reshape(devices * CAP, column_count)
-    back_up = back_up.reshape(devices * CAP, column_count)
+    summed, delta = lax.optimization_barrier((summed, delta))
+    back = lax.all_to_all(delta, ("gx", "gy"), split_axis=0, concat_axis=0, tiled=True)
+    back = back.reshape(devices * CAP, 2 * column_count)
     own_slot = lax.dynamic_slice_in_dim(slot_all, row_gx * block, block)
     own_rank = lax.dynamic_slice_in_dim(position, row_gx * block, block)
     pick = own_slot * CAP + own_rank
-    gate_value = gate_sum + back_gate[pick].astype(jnp.float32)
-    up_value = up_sum + back_up[pick].astype(jnp.float32)
+    picked = back[pick].astype(jnp.float32)
+    summed = summed.astype(jnp.float32)
+    gate_value = summed[:, :column_count] + picked[:, :column_count]
+    up_value = summed[:, column_count:] + picked[:, column_count:]
     return (jax.nn.silu(gate_value) * up_value).astype(jnp.bfloat16)
 
 

time: 365 us -> 398 us (1.090)
  waiting for transfers between devices: 228 us -> 256 us
  other arithmetic: 6.42 us -> 17.8 us
  matrix products: 35.1 us -> 29 us
    reduce_scatter x2 -> x1, waiting for transfers between devices: 90.7 us -> 127 us  [body(): summed = lax.psum_scatter(partial, 'gx', scatter_dimension=0, tiled=True)]
    optimization_barrier x0 -> x1, local copies, waits for them, and re-layouts: none -> 12.1 us  [body(): summed, delta = lax.optimization_barrier((summed, delta))]
    concatenate x0 -> x1, other arithmetic: none -> 8.93 us  [body(): jnp.concatenate([delta_gate.reshape(devices, CAP, column_count), delta_up...]
    all_to_all x1, waiting for transfers between devices: 17.3 us -> 9.58 us  [body(): lax.all_to_all(outgoing.reshape(devices, groups * CAP, tile_width), ('gx'...]
    reshape x3 -> x1, local copies, waits for them, and re-layouts: 19 us -> 12.3 us  [body(): back = back.reshape(devices * CAP, 2 * column_count)]
    dot_general x2 -> x1, matrix products: 28.1 us -> 23.8 us  [body(): jnp.dot(gathered, both_weights, preferred_element_type=jnp.float32)]
    convert_element_type x0 -> x2, other arithmetic: none -> 4.01 us  [the longest x1 2.09 us: body(): summed = summed.astype(jnp.float32)]
    all_to_all x2 -> x1, starting transfers between devices: 10.9 us -> 8.34 us  [body(): lax.all_to_all(delta, ('gx', 'gy'), split_axis=0, concat_axis=0, tiled=True)]
  transfers between devices with their start and end apart: 6 -> 4, of which waited for: 5 -> 4; matrix products, arithmetic and copies ran while one was open for 23% -> 12% of each run, Pallas kernels for 0% -> 0%
where the time goes in v2:
time: 398 us; the launch traced here: 396 us
  waiting for transfers between devices  256 us (64%)
  local copies, waits for them, and re-layouts  63.9 us (16%)
  matrix products  29 us (7%)
  other arithmetic  17.8 us (4%)
  starting transfers between devices  16.5 us (4%)
  between operations  13.5 us (3%)
    reduce_scatter x1, waiting for transfers between devices, body(): summed = lax.psum_scatter(partial, 'gx', scatter_dimension=0, tiled=True)  127 us
    all_to_all x1, waiting for transfers between devices, body(): lax.all_to_all(delta, ('gx', 'gy'), split_axis=0, concat_axis=0, tiled=True)  87.3 us
    all_gather x1, waiting for transfers between devices, body(): gathered = lax.all_gather(tokens, 'gy', axis=0, tiled=True)  30.6 us
    dot_general x1, matrix products, body(): jnp.dot(gathered, both_weights, preferred_element_type=jnp.float32)  23.8 us
    reshape x1, local copies, waits for them, and re-layouts, body(): back = back.reshape(devices * CAP, 2 * column_count)  12.3 us
    optimization_barrier x1, local copies, waits for them, and re-layouts, body(): summed, delta = lax.optimization_barrier((summed, delta))  12.1 us
    all_to_all x1, waiting for transfers between devices, body(): lax.all_to_all(outgoing.reshape(devices, groups * CAP, tile_width), ('gx'...  9.58 us
    concatenate x1, other arithmetic, body(): jnp.concatenate([delta_gate.reshape(devices, CAP, column_count), delta_up...  8.93 us
  transfers between devices with their start and end apart: 4, of which 4 were waited for; matrix products, arithmetic and copies ran while one was open for 12% of the time, Pallas kernels for 0%

profile of v2, /device:TPU:1, one launch (start us, length us, event | category | flops | bytes accessed | tf_op | source)
XLA Modules:
  0.0 396.2 jit_solution(12957413675771155715)
XLA Ops:
  6.5 0.0 copy-start
  6.5 0.0 all-gather.2.cloned.1.call-start
  6.5 0.7 all-gather.2.cloned.1.call-update
  7.3 0.0 reduce-scatter.2.cloned.1.call-start
  7.3 30.6 %all-gather.2.cloned.1.call-done = bf16[2048,512]{1,0:T(8,128)(2,1)} async-done(((bf16[256,512]{1,0:T(8,128)(2,1)}), bf16[2048,512]{1,0:T(8,128)(2,1)}) %all-gather.2.cloned.1.call-update) | async-done | bytes 2097168 | tf_op jit(solution)/shard_map/all_gather | solution.py:33
  37.9 23.8 %convert_bitcast_fusion = bf16[2048,7392]{1,0:T(8,128)(2,1)} fusion(bf16[2048,512]{1,0:T(8,128)(2,1)} %all-gather.2.cloned.1.call-done, bf16[512,3696]{0,1:T(8,128)(2,1)} %param.9, bf16[512,3696]{0,1:T(8,128)(2,1)} %param.8), kind=kOutput, calls=%fused_computation.2 | convolution fusion | flops 15532425216 | bytes 39944192 | tf_op jit(solution)/shard_map/dot_general | solution.py:36
  61.7 0.0 copy-start.5
  61.7 0.0 copy-start.6
  61.7 0.0 reduce-scatter.2.cloned.1.call-update
  61.7 0.7 copy-done.5
  62.4 0.0 copy-done.6
  62.4 0.6 select_reduce_fusion.1
  63.0 0.1 copy.39
  63.1 2.8 select_reduce_fusion
  65.9 0.1 copy.40
  66.0 0.1 compare_select_fusion
  66.1 3.0 scatter_custom_fusion
  69.1 8.2 %all-to-all-start = ((bf16[128,8,512]{2,1,0:T(8,128)(2,1)}), bf16[128,8,512]{2,1,0:T(8,128)(2,1)S(1)}, u32[]{:S(2)}, u32[]{:S(2)}) async-start(bf16[128,8,512]{2,1,0:T(8,128)(2,1)} %bitcast.42), calls=%async_computation.1 | async-start | bytes 2097152 | tf_op jit(solution)/shard_map/all_to_all | solution.py:52
  77.3 5.6 %fusion.23 = (bf16[1,64,29568]{2,1,0:T(8,128)(2,1)}, bf16[1,64,29568]{2,1,0:T(8,128)(2,1)}) fusion(bf16[1,128,29568]{2,1,0:T(8,128)(2,1)} %param.11), kind=kLoop, calls=%fused_computation.46 | loop fusion | bytes 15138816 | tf_op jit(solution)/shard_map/slice | solution.py:65
  82.8 7.5 %reshape_squeeze.11 = bf16[64,8,3696]{2,1,0:T(8,128)(2,1)} reshape(bf16[1,64,29568]{2,1,0:T(8,128)(2,1)} %get-tuple-element.10) | data formatting | bytes 7569408 | tf_op jit(solution)/shard_map/reshape;squeeze | solution.py:68
  90.4 7.5 %reshape_squeeze.10 = bf16[64,8,3696]{2,1,0:T(8,128)(2,1)} reshape(bf16[1,64,29568]{2,1,0:T(8,128)(2,1)} %get-tuple-element.9) | data formatting | bytes 7569408 | tf_op jit(solution)/shard_map/reshape;squeeze | solution.py:65
  97.9 9.6 %all-to-all-done = bf16[128,8,512]{2,1,0:T(8,128)(2,1)S(1)} async-done(((bf16[128,8,512]{2,1,0:T(8,128)(2,1)}), bf16[128,8,512]{2,1,0:T(8,128)(2,1)S(1)}, u32[]{:S(2)}, u32[]{:S(2)}) %all-to-all-start) | async-done | bytes 1048608 | tf_op jit(solution)/shard_map/all_to_all | solution.py:52
  107.5 0.0 copy-done
  107.5 0.5 fusion.15
  108.0 0.1 fusion.24
  108.1 0.0 copy-start.2
  108.1 3.5 fusion.4
  111.7 0.2 copy-done.2
  111.8 1.1 fusion.3
  113.0 3.7 copy_bitcast_fusion
  116.7 8.9 %pad_maximum_fusion = bf16[128,4,7392]{2,0,1:T(8,128)(2,1)} fusion(bf16[128,4,3696]{2,0,1:T(8,128)(2,1)} %get-tuple-element.13, bf16[128,4,3696]{2,0,1:T(8,128)(2,1)} %get-tuple-element.14), kind=kLoop, calls=%fused_computation.3 | loop fusion | flops 15138816 | bytes 15138816 | tf_op jit(solution)/shard_map/concatenate | solution.py:83
  125.6 127.4 %reduce-scatter.2.cloned.1.call-done = bf16[128,7392]{1,0:T(8,128)(2,1)} async-done(((bf16[2048,7392]{1,0:T(8,128)(2,1)}), bf16[128,7392]{1,0:T(8,128)(2,1)}) %reduce-scatter.2.cloned.1.call-update) | async-done | bytes 1892368 | tf_op jit(solution)/shard_map/reduce_scatter | solution.py:39
  253.0 12.1 %copy.47 = bf16[128,4,7392]{2,1,0:T(4,128)(2,1)} copy(bf16[128,4,7392]{2,0,1:T(8,128)(2,1)} %pad_maximum_fusion) | data formatting | bytes 15138816 | tf_op jit(solution)/shard_map/optimization_barrier | solution.py:86
  265.1 0.0 copy-start.4
  265.1 8.3 %all-to-all-start.1 = ((bf16[128,4,7392]{2,1,0:T(4,128)(2,1)}), bf16[128,4,7392]{2,1,0:T(4,128)(2,1)}, u32[]{:S(2)}, u32[]{:S(2)}) async-start(bf16[128,4,7392]{2,1,0:T(4,128)(2,1)} %copy.47), calls=%async_computation.2 | async-start | bytes 15204352 | tf_op jit(solution)/shard_map/all_to_all | solution.py:87
  273.5 0.1 compare_select_fusion.1
  273.6 0.0 copy-done.4
  273.6 2.1 convert_element_type.42
  275.7 87.3 %all-to-all-done.1 = bf16[128,4,7392]{2,1,0:T(4,128)(2,1)} async-done(((bf16[128,4,7392]{2,1,0:T(4,128)(2,1)}), bf16[128,4,7392]{2,1,0:T(4,128)(2,1)}, u32[]{:S(2)}, u32[]{:S(2)}) %all-to-all-start.1) | async-done | bytes 7569440 | tf_op jit(solution)/shard_map/all_to_all | solution.py:87
  362.9 12.3 %reshape.38 = bf16[512,7392]{1,0:T(8,128)(2,1)} reshape(bf16[128,4,7392]{2,1,0:T(4,128)(2,1)} %all-to-all-done.1) | data formatting | bytes 15138816 | tf_op jit(solution)/shard_map/reshape | solution.py:88
  375.2 8.9 %gather_fusion = bf16[128,7392]{1,0:T(8,128)(2,1)} fusion(bf16[512,7392]{1,0:T(8,128)(2,1)} %reshape.38, s32[1024]{0:T(1024)S(1)} %pad_clamp_fusion), kind=kCustom, calls=%fused_computation | custom fusion | bytes 3785216 | tf_op jit(solution)/shard_map/gather | solution.py:92
  384.1 0.0 copy-start.3
  384.1 0.0 copy-start.1
  384.1 1.9 convert_element_type.43
  386.1 0.7 copy-done.3
  386.8 1.3 fusion.10
  388.0 1.3 copy.48
  389.4 0.0 copy-done.1
  (1 shorter events, 0.0 us)
Async XLA Ops:
  6.5 101.0 %copy-start = (bf16[1,8192,128]{2,1,0:T(8,128)(2,1)S(1)}, bf16[1,8192,128]{2,1,0:T(8,128)(2,1)}, u32[]{:S(2)}) copy-start(bf16[1,8192,128]{2,1,0:T(8,128)(2,1)} %param.10) | copy-start | bytes 6291460
  6.5 31.4 %all-gather.2.cloned.1.call-start = ((), (), s32[]{:S(2)}) async-start(), calls=%async_computation.3 | async-start | bytes 2359296 | tf_op jit(solution)/shard_map/all_gather | solution.py:33
  7.3 245.8 %reduce-scatter.2.cloned.1.call-start = ((), (), s32[]{:S(2)}) async-start(), calls=%async_computation.4 | async-start | bytes 32309248 | tf_op jit(solution)/shard_map/reduce_scatter | solution.py:39
  61.7 0.7 copy-start.5
  61.7 0.7 copy-start.6
  69.1 38.4 %all-to-all-start = ((bf16[128,8,512]{2,1,0:T(8,128)(2,1)}), bf16[128,8,512]{2,1,0:T(8,128)(2,1)S(1)}, u32[]{:S(2)}, u32[]{:S(2)}) async-start(bf16[128,8,512]{2,1,0:T(8,128)(2,1)} %bitcast.42), calls=%async_computation.1 | async-start | bytes 2097152 | tf_op jit(solution)/shard_map/all_to_all | solution.py:52
  108.1 3.7 copy-start.2
  265.1 8.4 %copy-start.4 = (bf16[128,7392]{1,0:T(8,128)(2,1)S(1)}, bf16[128,7392]{1,0:T(8,128)(2,1)}, u32[]{:S(2)}) copy-start(bf16[128,7392]{1,0:T(8,128)(2,1)} %reduce-scatter.2.cloned.1.call-done) | copy-start | bytes 5677060
  265.1 97.8 %all-to-all-start.1 = ((bf16[128,4,7392]{2,1,0:T(4,128)(2,1)}), bf16[128,4,7392]{2,1,0:T(4,128)(2,1)}, u32[]{:S(2)}, u32[]{:S(2)}) async-start(bf16[128,4,7392]{2,1,0:T(4,128)(2,1)} %copy.47), calls=%async_computation.2 | async-start | bytes 15204352 | tf_op jit(solution)/shard_map/all_to_all | solution.py:87
  384.1 2.6 copy-start.3
  384.1 5.2 %copy-start.1 = (bf16[1,8192,128]{2,1,0:T(8,128)(2,1)S(1)}, bf16[1,8192,128]{2,1,0:T(8,128)(2,1)}, u32[]{:S(2)}) copy-start(bf16[1,8192,128]{2,1,0:T(8,128)(2,1)} %param.10) | copy-start | bytes 6291460
Sparse Core Ops, SparseCore 0:
  9.1 28.7 all-gather.1
  61.9 191.1 reduce-scatter.1
